TPU v7x, 512 devices: a whole 4x8x8 slice. The times are simulated.
512 devices in a mesh: seq: 128 (over y, z, core), tp: 4 (over x).
Axes of the slice: x: 4, y: 8, z: 8, core: 2. Of those that a mesh axis runs over, the one named last changes fastest.
Arguments:
- tokens: bfloat16 [32768, 1280], P('seq', 'tp'), may hold values from -6 to 6
- first_gain: float32 [1280], replicated, may hold values from 0.1 to 1.9
- w_query: bfloat16 [1280, 1280], P(None, 'tp')
- w_key: bfloat16 [1280, 1280], P(None, 'tp')
- w_value: bfloat16 [1280, 1280], P(None, 'tp'), may hold values from -0.15625 to 0.15625
- w_out: bfloat16 [1280, 1280], P('tp'), may hold values from -0.625 to 0.625
- segment_ids: int32 [32768], P('seq'), may hold values from 0 to 191, never falling along the last dimension, each value on 1 to 512 neighbouring positions
- keep_mask: int32 [32768], P('seq'), may hold values 0 or 1
- merge_gain: float32 [1280], replicated, may hold values from 0.1 to 1.9
- w_merge: bfloat16 [5120, 640], P('tp'), may hold values from -0.078125 to 0.078125
- merge_index: int32 [8192, 4], P('seq'), may hold values from 0 to 32767, as said below
- destination: int32 [8192], P('seq'), may hold values from 0 to 8191, as said below
Outputs:
- delivered: bfloat16 [8192, 640], P('seq', 'tp')
Inputs may be any that keep to these rules, and one draw needn't show every extreme that they name: `segment_ids`: segment numbers never fall along the tokens; each picture or clip holds 1 to 512 tokens and one holds exactly 512. `merge_index`: the four entries of merged row m are different tokens of the device that holds row m, that is of rows (m // 64) * 256 to that plus 256 - 1; every token lies in exactly one group. `destination`: a permutation of the merged rows. The owner of row m is destination[m] // 64; the 64 rows of each device go to exactly 32 owners, exactly 2 rows to each.
All inputs are finite; a program needn't handle non-finite values. No bound on the sum of `keep_mask` on one device may be relied on, other than what follows from the above.
Results may differ from a plain program's by a relative error of at most 0.022.
Values may be sent and summed in bfloat16 or wider, within the bound.
No kernel may reach another device: no remote copies, remote signals or barrier semaphores. Data moves between devices by JAX's collectives and lax.ppermute only.
A program may use at most 64 MiB of HBM per device.

v0:
```python
import jax
import jax.numpy as jnp
from jax import lax
from jax.sharding import PartitionSpec as P

HD = 80
EPS = 1e-06


def from_behind(shard, axis, by):
    length = lax.axis_size(axis)
    pairs = [(i, i + by) for i in range(length) if 0 <= i + by < length]
    return lax.ppermute(shard, axis, pairs)


def layer_norm(activations, norm_gain):
    activations = activations.astype(jnp.float32)
    row_mean = jnp.mean(activations, axis=-1, keepdims=True)
    centered = activations - row_mean
    variance = jnp.mean(centered * centered, axis=-1, keepdims=True)
    return centered * lax.rsqrt(variance + EPS) * norm_gain


def body(
    tokens,
    first_gain,
    w_query,
    w_key,
    w_value,
    w_out,
    segment_ids,
    keep_mask,
    merge_gain,
    w_merge,
    merge_index,
    destination,
):
    row_count = tokens.shape[0]
    local_width = w_query.shape[1]
    heads_here = local_width // HD
    gathered = lax.all_gather(tokens, "tp", axis=1, tiled=True)
    normed = layer_norm(gathered, first_gain).astype(jnp.bfloat16)
    queries = jnp.dot(normed, w_query, preferred_element_type=jnp.float32).astype(jnp.bfloat16)
    key_rows = jnp.dot(normed, w_key, preferred_element_type=jnp.float32).astype(jnp.bfloat16)
    value_rows = jnp.dot(normed, w_value, preferred_element_type=jnp.float32).astype(jnp.bfloat16)
    paired = jnp.concatenate([key_rows, value_rows], axis=1)
    code_query = segment_ids + 1
    code_key = jnp.where(keep_mask > 0, code_query, 0)
    pair_list = [paired]
    code_list = [code_key]
    for offset in (1, 2, -1, -2):
        moved_pair, moved_code = from_behind((paired, code_key), "seq", offset)
        pair_list.append(moved_pair)
        code_list.append(moved_code)
    all_pairs = jnp.concatenate(pair_list, axis=0)
    all_codes = jnp.concatenate(code_list, axis=0)
    window = all_pairs.shape[0]
    key_heads = all_pairs[:, :local_width].reshape(window, heads_here, HD)
    value_heads = all_pairs[:, local_width:].reshape(window, heads_here, HD)
    query_heads = queries.reshape(row_count, heads_here, HD)
    score_scale = HD ** (-0.5)
    scores = (
        jnp.einsum("qhd,khd->hqk", query_heads, key_heads, preferred_element_type=jnp.float32)
        * score_scale
    )
    query_pos = jnp.arange(row_count)[:, None]
    key_pos = jnp.arange(window)[None, :]
    allowed = (code_query[:, None] == all_codes[None, :]) | (key_pos == query_pos)
    scores = jnp.where(allowed[None], scores, -1e30)
    row_max = jnp.max(scores, axis=-1, keepdims=True)
    exponent = jnp.exp(scores - row_max)
    row_total = jnp.sum(exponent, axis=-1, keepdims=True)
    weights = (exponent / row_total).astype(jnp.bfloat16)
    attended = jnp.einsum("hqk,khd->qhd", weights, value_heads, preferred_element_type=jnp.float32)
    attended = attended.reshape(row_count, local_width).astype(jnp.bfloat16)
    partial_sum = jnp.dot(attended, w_out, preferred_element_type=jnp.float32)
    position = lax.axis_index("tp")
    seq_index = lax.axis_index("seq")
    local_index = merge_index - seq_index * row_count
    column = lax.dynamic_slice_in_dim(local_index, position, 1, 1)[:, 0]
    mixed_sum = lax.psum(partial_sum.astype(jnp.bfloat16), "tp").astype(jnp.float32)
    updated = gathered.astype(jnp.float32) + mixed_sum
    merged_norm = layer_norm(updated, merge_gain).astype(jnp.bfloat16)
    picked = jnp.take(merged_norm, column, axis=0)
    partial_proj = jnp.dot(picked, w_merge, preferred_element_type=jnp.float32)
    projected = lax.psum_scatter(
        partial_proj.astype(jnp.bfloat16), "tp", scatter_dimension=1, tiled=True
    )
    slot_count = projected.shape[0]
    slot_range = jnp.arange(slot_count)
    piece_rows = lax.all_gather(projected, "seq", axis=0, tiled=True)
    piece_dest = lax.all_gather(destination, "seq", axis=0, tiled=True)
    piece_slot = piece_dest - seq_index * slot_count
    one_hot = (piece_slot[None, :] == slot_range[:, None]).astype(jnp.bfloat16)
    delivered = jnp.dot(one_hot, piece_rows, preferred_element_type=jnp.float32)
    return delivered.astype(jnp.bfloat16)


def solution(mesh):
    return jax.shard_map(
        body,
        mesh=mesh,
        in_specs=(
            P("seq", "tp"),
            P(),
            P(None, "tp"),
            P(None, "tp"),
            P(None, "tp"),
            P("tp", None),
            P("seq"),
            P("seq"),
            P(),
            P("tp", None),
            P("seq", None),
            P("seq"),
        ),
        out_specs=P("seq", "tp"),
        check_vma=False,
    )
```

profile of v0, /device:TPU:2, one launch (start us, length us, event | category | flops | bytes accessed | tf_op | source)
XLA Modules:
  0.0 674.0 jit_solution(445219230451714577)
XLA Ops:
  6.5 16.1 %all_gather.10 = bf16[256,1280]{0,1:T(8,128)(2,1)S(1)} all-gather(bf16[256,320]{0,1:T(8,128)(2,1)} %param.12), channel_id=1, replica_groups=mesh['seq'=128,'tp'=4] {'tp'}, dimensions={1}, use_global_device_ids=true | all-gather | bytes 819200 | tf_op jit(solution)/shard_map/all_gather | solution.py:41
  23.4 0.6 copy-done.10
  24.0 0.5 convolution_convert_fusion.3
  24.6 0.5 convolution_convert_fusion.2
  25.1 1.0 pad_maximum_fusion
  26.1 2.0 collective-permute-start
  28.1 2.2 collective-permute-start.1
  30.3 1.3 collective-permute-start.2
  31.6 1.3 collective-permute-start.3
  32.9 4.9 collective-permute-start.4
  37.8 2.3 convolution_convert_fusion.1
  40.2 4.9 collective-permute-start.5
  45.0 1.3 collective-permute-done.5
  46.3 1.3 collective-permute-start.6
  47.6 2.1 collective-permute-done.6
  49.7 1.3 collective-permute-start.7
  51.0 5.7 collective-permute-done.7
  56.8 1.0 fusion.13
  57.8 1.0 constant_dynamic-update-slice_fusion.3
  58.9 1.0 fusion.35
  59.9 3.1 exponential_reduce_fusion
  63.1 4.5 fusion.16
  67.6 2.3 convolution_convert_fusion
  70.0 65.5 %all-reduce.3.cloned.1.call-done = bf16[256,1280]{1,0:T(8,128)(2,1)} async-done(((bf16[256,1280]{1,0:T(8,128)(2,1)}), bf16[256,1280]{1,0:T(8,128)(2,1)}) %all-reduce.3.cloned.1.call-update) | async-done | bytes 655376 | tf_op jit(solution)/shard_map/psum | solution.py:81
  135.6 1.4 fusion.15
  137.7 0.7 gather_fusion
  138.9 0.8 copy.15
  139.8 26.4 %reduce-scatter.4.cloned.1.call-done = bf16[160,64]{1,0:T(8,128)(2,1)} async-done(((bf16[640,64]{1,0:T(8,128)(2,1)}), bf16[160,64]{1,0:T(8,128)(2,1)}) %reduce-scatter.4.cloned.1.call-update) | async-done | bytes 20496
  166.1 1.5 copy.16
  167.6 1.3 dynamic-slice
  169.9 494.1 %all-reduce = s32[8192]{0:T(1024)S(1)} all-reduce(s32[8192]{0:T(1024)S(1)} %dynamic-update-slice), channel_id=1, replica_groups=mesh['seq'=128,'tp'=4] {'seq'}, use_global_device_ids=true, to_apply=%add | all-reduce | flops 8192 | bytes 65536
  664.0 3.5 fusion.17
  (64 shorter events, 2.5 us)
Async XLA Ops:
  6.5 131.9 %copy-start = (bf16[1280,640]{1,0:T(8,128)(2,1)S(1)}, bf16[1280,640]{1,0:T(8,128)(2,1)}, u32[]{:S(2)}) copy-start(bf16[1280,640]{1,0:T(8,128)(2,1)} %param.21) | copy-start | bytes 4915204
  6.5 129.0 %all-reduce.3.cloned.1.call-start = ((), (), s32[]{:S(2)}) async-start(), calls=%async_computation.1 | async-start | bytes 1310720 | tf_op jit(solution)/shard_map/psum | solution.py:81
  22.6 0.8 copy-start.12
  22.9 1.1 copy-start.10
  23.4 1.2 copy-start.11
  24.6 8.3 %copy-start.8 = (s32[256]{0:T(256)S(1)}, s32[256]{0:T(256)}, u32[]{:S(2)}) copy-start(s32[256]{0:T(256)} %param.18) | copy-start | bytes 3076
  24.6 8.3 %copy-start.9 = (s32[256]{0:T(256)S(1)}, s32[256]{0:T(256)}, u32[]{:S(2)}) copy-start(s32[256]{0:T(256)} %param.19) | copy-start | bytes 3076
  26.1 31.7 %collective-permute-start = (bf16[256,640]{0,1:T(8,128)(2,1)}, bf16[256,640]{0,1:T(8,128)(2,1)}, u32[]{:S(2)}, u32[]{:S(2)}) collective-permute-start(bf16[256,640]{0,1:T(8,128)(2,1)} %get-tuple-element.11), channel_id=1, source_target_pairs={{0,4},{4,8},{8,12},{12,16},{16,20},{20,24},{24,28},{28,32},{32,36}... | collective-permute-start | bytes 983048 | tf_op jit(solution)/shard_map/ppermute | solution.py:13
  28.1 30.7 %collective-permute-start.1 = (bf16[256,640]{0,1:T(8,128)(2,1)}, bf16[256,640]{0,1:T(8,128)(2,1)S(1)}, u32[]{:S(2)}, u32[]{:S(2)}) collective-permute-start(bf16[256,640]{0,1:T(8,128)(2,1)} %get-tuple-element.11), channel_id=1, source_target_pairs={{0,8},{4,12},{8,16},{12,20},{16,24},{20,28},{24,32},{28,36},{32,40... | collective-permute-start | bytes 983048 | tf_op jit(solution)/shard_map/ppermute | solution.py:13
  30.3 28.5 %collective-permute-start.2 = (bf16[256,640]{0,1:T(8,128)(2,1)}, bf16[256,640]{0,1:T(8,128)(2,1)S(1)}, u32[]{:S(2)}, u32[]{:S(2)}) collective-permute-start(bf16[256,640]{0,1:T(8,128)(2,1)} %get-tuple-element.11), channel_id=1, source_target_pairs={{4,0},{8,4},{12,8},{16,12},{20,16},{24,20},{28,24},{32,28},{36,32}... | collective-permute-start | bytes 983048 | tf_op jit(solution)/shard_map/ppermute | solution.py:13
  31.6 27.3 %collective-permute-start.3 = (bf16[256,640]{0,1:T(8,128)(2,1)}, bf16[256,640]{0,1:T(8,128)(2,1)S(1)}, u32[]{:S(2)}, u32[]{:S(2)}) collective-permute-start(bf16[256,640]{0,1:T(8,128)(2,1)} %get-tuple-element.11), channel_id=1, source_target_pairs={{8,0},{12,4},{16,8},{20,12},{24,16},{28,20},{32,24},{36,28},{40,32... | collective-permute-start | bytes 983048 | tf_op jit(solution)/shard_map/ppermute | solution.py:13
  32.9 24.9 %copy-start.2 = (bf16[1280,640]{0,1:T(8,128)(2,1)S(1)}, bf16[1280,640]{0,1:T(8,128)(2,1)}, u32[]{:S(2)}) copy-start(bf16[1280,640]{0,1:T(8,128)(2,1)} %get-tuple-element.12) | copy-start | bytes 4915204
  32.9 7.2 %collective-permute-start.4 = (s32[256]{0:T(256)S(1)}, s32[256]{0:T(256)S(1)}, u32[]{:S(2)}, u32[]{:S(2)}) collective-permute-start(s32[256]{0:T(256)S(1)} %get-tuple-element.8), channel_id=1, source_target_pairs={{0,4},{4,8},{8,12},{12,16},{16,20},{20,24},{24,28},{28,32},{32,36}... | collective-permute-start | bytes 3080 | tf_op jit(solution)/shard_map/ppermute | solution.py:13
  40.2 6.1 collective-permute-start.5
  46.3 3.4 collective-permute-start.6
  49.7 7.0 %collective-permute-start.7 = (s32[256]{0:T(256)S(1)}, s32[256]{0:T(256)S(1)}, u32[]{:S(2)}, u32[]{:S(2)}) collective-permute-start(s32[256]{0:T(256)S(1)} %get-tuple-element.8), channel_id=1, source_target_pairs={{8,0},{12,4},{16,8},{20,12},{24,16},{28,20},{32,24},{36,28},{40,32... | collective-permute-start | bytes 3080 | tf_op jit(solution)/shard_map/ppermute | solution.py:13
  58.9 1.0 copy-start.5
  59.9 3.1 copy-start.4
  63.1 4.5 copy-start.3
  67.6 2.4 copy-start.7
  69.9 96.2 %reduce-scatter.4.cloned.1.call-start = ((), (), s32[]{:S(2)}) async-start(), calls=%async_computation.3 | async-start | bytes 204800
  70.0 67.3 %copy-start.6 = (f32[1280]{0:T(1024)S(1)}, f32[1280]{0:T(1024)}, u32[]{:S(2)}) copy-start(f32[1280]{0:T(1024)} %param.20) | copy-start | bytes 15364
  135.6 1.4 copy-start.1
  138.4 31.2 %copy-start.13 = (s32[64]{0:T(128)S(1)}, s32[64]{0:T(128)}, u32[]{:S(2)}) copy-start(s32[64]{0:T(128)} %param.23) | copy-start | bytes 772
  139.7 524.2 %all-gather.2.cloned.1.call-start = ((), (), s32[]{:S(2)}) async-start(), calls=%async_computation.2 | async-start | bytes 4227072 | tf_op jit(solution)/shard_map/all_gather | solution.py:91
Sparse Core Ops, SparseCore 0:
  70.0 65.4 all-reduce.2
  139.8 26.2 reduce-scatter.3
  169.3 85.4 all-gather.1
where the time goes:
time: 675 us; the launch traced here: 674 us
  blocking collectives  510 us (76%)
  waiting for transfers between devices  101 us (15%)
  starting transfers between devices  19.1 us (3%)
  matrix products  17.3 us (3%)
  between operations  14.1 us (2%)
  local copies, waits for them, and re-layouts  7.64 us (1%)
    unnamed x1, blocking collectives  494 us
    psum x1, waiting for transfers between devices, body(): lax.psum(partial_sum.astype(jnp.bfloat16), 'tp').astype(jnp.float32)  65.5 us
    unnamed x4, waiting for transfers between devices  26.4 us
    ppermute x8, starting transfers between devices, from_behind(): return lax.ppermute(shard, axis, pairs)  19.1 us
    all_gather x1, blocking collectives, body(): gathered = lax.all_gather(tokens, 'tp', axis=1, tiled=True)  16.1 us
  transfers between devices with their start and end apart: 11, of which 5 were waited for; matrix products, arithmetic and copies ran while one was open for 1% of the time, Pallas kernels for 0%

commit v1 on v0

--- a/solution.py
+++ b/solution.py
@@ -5,6 +5,11 @@
 
 HD = 80
 EPS = 1e-06
+
+
+def exchange_gather(array, mesh_axis, dim):
+    stack = jnp.stack([array] * lax.axis_size(mesh_axis))
+    return jnp.concatenate(lax.all_to_all(stack, mesh_axis, 0, 0), axis=dim)
 
 
 def from_behind(shard, axis, by):
@@ -38,7 +43,7 @@
     row_count = tokens.shape[0]
     local_width = w_query.shape[1]
     heads_here = local_width // HD
-    gathered = lax.all_gather(tokens, "tp", axis=1, tiled=True)
+    gathered = exchange_gather(tokens, "tp", 1)
     normed = layer_norm(gathered, first_gain).astype(jnp.bfloat16)
     queries = jnp.dot(normed, w_query, preferred_element_type=jnp.float32).astype(jnp.bfloat16)
     key_rows = jnp.dot(normed, w_key, preferred_element_type=jnp.float32).astype(jnp.bfloat16)

time: 675 us -> 664 us (0.984)
  blocking collectives: 510 us -> 494 us
    all_gather x1 -> x0, blocking collectives: 16.1 us -> none  [body(): gathered = lax.all_gather(tokens, 'tp', axis=1, tiled=True)]
    psum x1, waiting for transfers between devices: 65.5 us -> 52 us  [body(): lax.psum(partial_sum.astype(jnp.bfloat16), 'tp').astype(jnp.float32)]
    ppermute x8, waiting for transfers between devices: 9.14 us -> 19.8 us  [from_behind(): return lax.ppermute(shard, axis, pairs)]
    all_to_all x0 -> x1, starting transfers between devices: none -> 9.33 us  [exchange_gather(): return jnp.concatenate(lax.all_to_all(stack, mesh_axis, 0, 0), axis=dim)]
  transfers between devices with their start and end apart: 11 -> 12, of which waited for: 5 -> 6; matrix products, arithmetic and copies ran while one was open for 1% -> 1% of each run, Pallas kernels for 0% -> 0%
where the time goes in v1:
time: 664 us; the launch traced here: 663 us
  blocking collectives  494 us (74%)
  waiting for transfers between devices  98.2 us (15%)
  starting transfers between devices  24.6 us (4%)
  matrix products  15.8 us (2%)
  between operations  14.1 us (2%)
  local copies, waits for them, and re-layouts  11.1 us (2%)
    unnamed x1, blocking collectives  494 us
    psum x1, waiting for transfers between devices, body(): lax.psum(partial_sum.astype(jnp.bfloat16), 'tp').astype(jnp.float32)  52 us
    unnamed x4, waiting for transfers between devices  26.4 us
    ppermute x8, waiting for transfers between devices, from_behind(): return lax.ppermute(shard, axis, pairs)  19.8 us
    ppermute x8, starting transfers between devices, from_behind(): return lax.ppermute(shard, axis, pairs)  15.2 us
  transfers between devices with their start and end apart: 12, of which 6 were waited for; matrix products, arithmetic and copies ran while one was open for 1% of the time, Pallas kernels for 0%

profile of v1, /device:TPU:2, one launch (start us, length us, event | category | flops | bytes accessed | tf_op | source)
XLA Modules:
  0.0 663.0 jit_solution(6816031242047209145)
XLA Ops:
  6.5 1.9 stack.2
  8.5 9.3 %all-to-all-start = ((bf16[4,256,320]{1,2,0:T(8,128)(2,1)}), bf16[4,256,320]{1,2,0:T(8,128)(2,1)S(1)}, u32[]{:S(2)}, u32[]{:S(2)}) async-start(bf16[4,256,320]{1,2,0:T(8,128)(2,1)} %stack.2), calls=%async_computation | async-start | bytes 1310720 | tf_op jit(solution)/shard_map/all_to_all | solution.py:12
  17.8 1.4 collective-permute-start.4
  19.3 1.3 collective-permute-start.5
  20.6 1.3 collective-permute-start.6
  21.9 1.3 collective-permute-start.7
  23.2 1.2 collective-permute-done.6
  24.4 4.4 collective-permute-done.7
  30.0 0.5 copy-done.3
  30.9 2.0 collective-permute-start
  33.2 5.3 collective-permute-start.1
  38.5 1.3 collective-permute-start.2
  39.8 1.3 collective-permute-start.3
  41.1 1.1 convolution_convert_fusion.1
  42.2 2.7 collective-permute-done.1
  45.0 11.4 %collective-permute-done.3 = bf16[256,640]{0,1:T(8,128)(2,1)S(1)} collective-permute-done((bf16[256,640]{0,1:T(8,128)(2,1)S(1)}, bf16[256,640]{0,1:T(8,128)(2,1)S(1)}, u32[]{:S(2)}, u32[]{:S(2)}) %collective-permute-start.3) | collective-permute-done | bytes 327712 | tf_op jit(solution)/shard_map/ppermute | solution.py:18
  56.4 1.0 fusion.26
  57.4 3.1 exponential_reduce_fusion
  60.6 4.5 fusion.9
  65.1 2.3 convolution_convert_fusion
  67.6 1.2 convert_element_type.73
  68.7 1.7 copy.15
  70.5 52.0 %all-reduce.3.cloned.1.call-done = bf16[256,1280]{1,0:T(8,128)(2,1)} async-done(((bf16[256,1280]{1,0:T(8,128)(2,1)}), bf16[256,1280]{1,0:T(8,128)(2,1)}) %all-reduce.3.cloned.1.call-update) | async-done | bytes 655376 | tf_op jit(solution)/shard_map/psum | solution.py:86
  122.5 1.4 fusion.14
  124.2 1.1 multiply_convert_fusion
  125.4 2.0 gather_fusion
  127.9 0.8 copy.16
  128.7 26.4 %reduce-scatter.4.cloned.1.call-done = bf16[160,64]{1,0:T(8,128)(2,1)} async-done(((bf16[640,64]{1,0:T(8,128)(2,1)}), bf16[160,64]{1,0:T(8,128)(2,1)}) %reduce-scatter.4.cloned.1.call-update) | async-done | bytes 20496
  155.1 1.5 copy.17
  156.6 1.3 dynamic-slice
  158.8 494.2 %all-reduce = s32[8192]{0:T(1024)S(1)} all-reduce(s32[8192]{0:T(1024)S(1)} %dynamic-update-slice), channel_id=1, replica_groups=mesh['seq'=128,'tp'=4] {'seq'}, use_global_device_ids=true, to_apply=%add | all-reduce | flops 8192 | bytes 65536
  653.0 3.5 fusion.10
  (66 shorter events, 3.2 us)
Async XLA Ops:
  6.5 120.9 %copy-start = (bf16[1280,640]{1,0:T(8,128)(2,1)S(1)}, bf16[1280,640]{1,0:T(8,128)(2,1)}, u32[]{:S(2)}) copy-start(bf16[1280,640]{1,0:T(8,128)(2,1)} %param.21) | copy-start | bytes 4915204
  6.5 11.3 %copy-start.10 = (s32[256]{0:T(256)S(1)}, s32[256]{0:T(256)}, u32[]{:S(2)}) copy-start(s32[256]{0:T(256)} %param.18) | copy-start | bytes 3076
  6.5 11.3 %copy-start.11 = (s32[256]{0:T(256)S(1)}, s32[256]{0:T(256)}, u32[]{:S(2)}) copy-start(s32[256]{0:T(256)} %param.19) | copy-start | bytes 3076
  6.5 22.8 %copy-start.7 = (f32[1280]{0:T(1024)S(1)}, f32[1280]{0:T(1024)}, u32[]{:S(2)}) copy-start(f32[1280]{0:T(1024)} %param.13) | copy-start | bytes 15364
  8.5 20.4 %all-to-all-start = ((bf16[4,256,320]{1,2,0:T(8,128)(2,1)}), bf16[4,256,320]{1,2,0:T(8,128)(2,1)S(1)}, u32[]{:S(2)}, u32[]{:S(2)}) async-start(bf16[4,256,320]{1,2,0:T(8,128)(2,1)} %stack.2), calls=%async_computation | async-start | bytes 1310720 | tf_op jit(solution)/shard_map/all_to_all | solution.py:12
  17.8 11.8 %copy-start.2 = (bf16[1280,320]{0,1:T(8,128)(2,1)S(1)}, bf16[1280,320]{0,1:T(8,128)(2,1)}, u32[]{:S(2)}) copy-start(bf16[1280,320]{0,1:T(8,128)(2,1)} %param.16) | copy-start | bytes 2457604
  17.8 104.7 %all-reduce.3.cloned.1.call-start = ((), (), s32[]{:S(2)}) async-start(), calls=%async_computation.2 | async-start | bytes 1310720 | tf_op jit(solution)/shard_map/psum | solution.py:86
  17.8 5.3 collective-permute-start.4
  19.3 3.9 collective-permute-start.5
  20.6 3.9 collective-permute-start.6
  21.9 7.0 %collective-permute-start.7 = (s32[256]{0:T(256)S(1)}, s32[256]{0:T(256)S(1)}, u32[]{:S(2)}, u32[]{:S(2)}) collective-permute-start(s32[256]{0:T(256)S(1)} %get-tuple-element.8), channel_id=1, source_target_pairs={{8,0},{12,4},{16,8},{20,12},{24,16},{28,20},{32,24},{36,28},{40,32... | collective-permute-start | bytes 3080 | tf_op jit(solution)/shard_map/ppermute | solution.py:18
  29.3 1.1 copy-start.3
  30.4 10.6 %copy-start.4 = (bf16[1280,320]{0,1:T(8,128)(2,1)S(1)}, bf16[1280,320]{0,1:T(8,128)(2,1)}, u32[]{:S(2)}) copy-start(bf16[1280,320]{0,1:T(8,128)(2,1)} %param.14) | copy-start | bytes 2457604
  30.9 11.2 %collective-permute-start = (bf16[256,640]{0,1:T(8,128)(2,1)S(1)}, bf16[256,640]{0,1:T(8,128)(2,1)S(1)}, u32[]{:S(2)}, u32[]{:S(2)}) collective-permute-start(bf16[256,640]{0,1:T(8,128)(2,1)S(1)} %get-tuple-element.11), channel_id=1, source_target_pairs={{0,4},{4,8},{8,12},{12,16},{16,20},{20,24},{24,28},{28,32},{32,36}... | collective-permute-start | bytes 983048 | tf_op jit(solution)/shard_map/ppermute | solution.py:18
  33.2 11.7 %collective-permute-start.1 = (bf16[256,640]{0,1:T(8,128)(2,1)S(1)}, bf16[256,640]{0,1:T(8,128)(2,1)S(1)}, u32[]{:S(2)}, u32[]{:S(2)}) collective-permute-start(bf16[256,640]{0,1:T(8,128)(2,1)S(1)} %get-tuple-element.11), channel_id=1, source_target_pairs={{0,8},{4,12},{8,16},{12,20},{16,24},{20,28},{24,32},{28,36},{32,40... | collective-permute-start | bytes 983048 | tf_op jit(solution)/shard_map/ppermute | solution.py:18
  38.5 6.5 collective-permute-start.2
  39.8 16.6 %collective-permute-start.3 = (bf16[256,640]{0,1:T(8,128)(2,1)S(1)}, bf16[256,640]{0,1:T(8,128)(2,1)S(1)}, u32[]{:S(2)}, u32[]{:S(2)}) collective-permute-start(bf16[256,640]{0,1:T(8,128)(2,1)S(1)} %get-tuple-element.11), channel_id=1, source_target_pairs={{8,0},{12,4},{16,8},{20,12},{24,16},{28,20},{32,24},{36,28},{40,32... | collective-permute-start | bytes 983048 | tf_op jit(solution)/shard_map/ppermute | solution.py:18
  57.4 3.1 copy-start.6
  60.5 4.5 copy-start.5
  65.1 2.4 copy-start.9
  67.4 87.7 %reduce-scatter.4.cloned.1.call-start = ((), (), s32[]{:S(2)}) async-start(), calls=%async_computation.4 | async-start | bytes 204800
  70.5 53.7 %copy-start.8 = (f32[1280]{0:T(1024)S(1)}, f32[1280]{0:T(1024)}, u32[]{:S(2)}) copy-start(f32[1280]{0:T(1024)} %param.20) | copy-start | bytes 15364
  122.5 1.4 copy-start.1
  125.3 33.2 %copy-start.12 = (s32[64]{0:T(128)S(1)}, s32[64]{0:T(128)}, u32[]{:S(2)}) copy-start(s32[64]{0:T(128)} %param.23) | copy-start | bytes 772
  128.7 524.3 %all-gather.2.cloned.1.call-start = ((), (), s32[]{:S(2)}) async-start(), calls=%async_computation.3 | async-start | bytes 4227072 | tf_op jit(solution)/shard_map/all_gather | solution.py:96
Sparse Core Ops, SparseCore 0:
  67.6 54.8 all-reduce.2
  128.8 26.2 reduce-scatter.3
  158.2 85.5 all-gather.1
